TPU v7x, 128 devices: a whole 4x4x4 slice. The times are simulated.
128 devices in a mesh: space: 32 (over y, x, core), shell: 4 (over z).
Axes of the slice: x: 4, y: 4, z: 4, core: 2. Of those that a mesh axis runs over, the one named last changes fastest.
Arguments:
- weights: float32 [262144], P(('space', 'shell')), may hold values from 0.02 to 1.5
- seg_streamline: int32 [32, 4, 32, 256], P('space', 'shell'), may hold values from 0 to 2047
- seg_features: float32 [32, 4, 32, 256, 128], P('space', 'shell'), may hold values from -12 to 12
- pair_counts: int32 [32, 4, 32], P('space', 'shell'), may hold values from 32 to 256, as said below
- seg_voxel: int32 [32, 4, 32, 256], P('space', 'shell'), may hold values from 0 to 4095
- dictionary: float32 [128, 256], P(None, 'shell'), may hold values from -0.375 to 0.375
- measured: float32 [256, 131072], P('shell', 'space'), may hold values from -6 to 6
Outputs:
- new_weights: float32 [262144], P(('space', 'shell'))
- residual: float32 [256, 131072], P('shell', 'space')
Inputs may be any that keep to these rules, and one draw needn't show every extreme that they name: In each shell group q one voxel block d has pair_counts[s, q, d] = 256 for every s.
All inputs are finite; a program needn't handle non-finite values.
Results may differ from a plain program's by a relative error of at most 0.0003.
Values sent between devices are 32-bit elements; how exact they have to be, the bound alone decides.
No kernel may reach another device: no remote copies, remote signals or barrier semaphores. Data moves between devices by JAX's collectives and lax.ppermute only.
A program may use at most 64 MiB of HBM per device.

v0:
```python
import jax
import jax.numpy as jnp
from jax import lax
from jax.sharding import PartitionSpec as P

ITERS = 2
HI = lax.Precision.HIGHEST


def one_hot_pair(index, count):
    low_count = 64
    high_count = count // low_count
    flat = index.reshape(-1)
    high = (flat // low_count)[:, None] == lax.broadcasted_iota(jnp.int32, (1, high_count), 1)
    low = (flat % low_count)[:, None] == lax.broadcasted_iota(jnp.int32, (1, low_count), 1)
    return (high.astype(jnp.float32), low.astype(jnp.float32))


def pick(table, high, low):
    rows = jnp.dot(high, table.reshape(high.shape[1], low.shape[1]), precision=HI)
    return jnp.sum(rows * low, axis=1)


def spread(values, high, low):
    return jnp.dot(high.T, values.reshape(-1)[:, None] * low, precision=HI).reshape(-1)


def on_device(weights, seg_streamline, seg_features, pair_counts, seg_voxel, dictionary, measured):
    blocks = seg_streamline.shape[2]
    slots = seg_streamline.shape[3]
    coeffs = seg_features.shape[4]
    streams = weights.shape[0]
    stream_index = seg_streamline.reshape(blocks, slots)
    voxel_index = seg_voxel.reshape(blocks * slots)
    counts = pair_counts.reshape(blocks)
    live_slot = lax.broadcasted_iota(jnp.int32, (blocks, slots), 1) < counts[:, None]
    masked = jnp.where(
        live_slot[:, :, None], seg_features.reshape(blocks, slots, coeffs), jnp.float32(0.0)
    )
    half = slots // 2
    feat_parts = [
        lax.all_to_all(masked[:, h * half : (h + 1) * half], "space", 0, 0, tiled=True)
        for h in range(2)
    ]
    gram = lax.psum(jnp.dot(dictionary, dictionary.T, precision=HI), "shell")
    data_proj = lax.psum(jnp.dot(measured.T, dictionary.T, precision=HI), "shell")
    feat_parts[1], gram, data_proj = lax.optimization_barrier((feat_parts[1], gram, data_proj))
    vox_parts = [
        voxel_index.reshape(blocks, slots)[:, h * half : (h + 1) * half].reshape(-1)
        for h in range(2)
    ]
    local_feat = jnp.concatenate(feat_parts, axis=1).reshape(blocks * slots, coeffs)
    high, low = one_hot_pair(stream_index, streams)
    column_sq = spread(jnp.sum(masked * masked, axis=2), high, low)
    scaling = 0.5 / (0.5 + column_sq)
    current = weights
    residual = jnp.zeros(measured.shape, jnp.float32)
    for iteration in range(ITERS):
        picked = pick(current, high, low).reshape(blocks, slots)
        local_x = lax.all_to_all(picked, "space", split_axis=0, concat_axis=0, tiled=True)
        partial_coeff = jnp.zeros((measured.shape[1], coeffs), jnp.float32)
        for h in range(2):
            part_x = local_x[:, h * half : (h + 1) * half].reshape(-1, 1)
            partial_coeff = partial_coeff.at[vox_parts[h]].add(
                part_x * feat_parts[h].reshape(-1, coeffs)
            )
        coeff_sum = lax.psum(partial_coeff, "shell")
        if iteration == ITERS - 1:
            residual = jnp.einsum("jg,vj->gv", dictionary, coeff_sum, precision=HI) - measured
        adjoint = jnp.dot(coeff_sum, gram, precision=HI) - data_proj
        local_grad = jnp.sum(local_feat * adjoint[voxel_index], axis=1).reshape(blocks, slots)
        grad_slot = lax.all_to_all(local_grad, "space", split_axis=0, concat_axis=0, tiled=True)
        gradient = spread(grad_slot, high, low)
        current = jnp.maximum(current - scaling * gradient, 0.0)
    return (current, residual)


def solution(mesh):
    in_specs = (
        P(("space", "shell")),
        P("space", "shell", None, None),
        P("space", "shell", None, None, None),
        P("space", "shell", None),
        P("space", "shell", None, None),
        P(None, "shell"),
        P("shell", "space"),
    )
    out_specs = (P(("space", "shell")), P("shell", "space"))
    return jax.shard_map(
        on_device, mesh=mesh, in_specs=in_specs, out_specs=out_specs, check_vma=False
    )
```

profile of v0, /device:TPU:1, one launch (start us, length us, event | category | flops | bytes accessed | tf_op | source)
XLA Modules:
  0.0 421.6 jit_solution(4449629302932283)
XLA Ops:
  10.6 8.6 %all-to-all-start.2 = ((f32[32,1,256]{2,1,0:T(1,128)}), f32[32,1,256]{2,1,0:T(1,128)S(1)}, u32[]{:S(2)}, u32[]{:S(2)}) async-start(f32[32,1,256]{2,1,0:T(1,128)} %bitcast.6), calls=%async_computation.2 | async-start | bytes 65536 | tf_op jit(solution)/shard_map/all_to_all | solution.py:60
  19.3 4.5 %multiply_reduce_fusion = (f32[32,256]{1,0:T(8,128)S(1)}, f32[32,256,128]{2,1,0:T(8,128)S(1)}) fusion(f32[1,1,32,256,128]{4,3,2,1,0:T(8,128)} %param.9, pred[32,256]{1,0:T(8,128)(4,1)S(1)} %iota_compare_fusion.10), kind=kLoop, calls=%fused_computation.18 | loop fusion | flops 3137536 | bytes 8429568 | tf_op jit(solution)/shard_map/reduce_sum | solution.py:54
  26.5 7.1 %all-to-all-start = ((f32[32,128,128]{2,1,0:T(8,128)}), f32[32,128,128]{2,1,0:T(8,128)S(1)}, u32[]{:S(2)}, u32[]{:S(2)}) async-start(f32[32,128,128]{2,1,0:T(8,128)} %get-tuple-element.12), calls=%async_computation | async-start | bytes 4194304 | tf_op jit(solution)/shard_map/all_to_all | solution.py:42
  34.5 4.8 %fusion.49 = f32[4096,128]{1,0:T(8,128)} fusion(f32[64,4096]{1,0:T(8,128)S(1)} %copy-done.6, f32[128,64]{0,1:T(8,128)S(1)} %copy-done), kind=kOutput, calls=%fused_computation.82 | convolution fusion | flops 402653184 | bytes 3178496 | tf_op jit(solution)/shard_map/dot_general | solution.py:46
  39.4 21.9 %all-to-all-done = f32[32,128,128]{2,1,0:T(8,128)S(1)} async-done(((f32[32,128,128]{2,1,0:T(8,128)}), f32[32,128,128]{2,1,0:T(8,128)S(1)}, u32[]{:S(2)}, u32[]{:S(2)}) %all-to-all-start) | async-done | bytes 2097184 | tf_op jit(solution)/shard_map/all_to_all | solution.py:42
  61.4 6.7 %all-to-all-start.1 = ((f32[32,128,128]{2,1,0:T(8,128)}), f32[32,128,128]{2,1,0:T(8,128)}, u32[]{:S(2)}, u32[]{:S(2)}) async-start(f32[32,128,128]{2,1,0:T(8,128)} %get-tuple-element.13), calls=%async_computation.1 | async-start | bytes 4194304 | tf_op jit(solution)/shard_map/all_to_all | solution.py:42
  70.2 23.2 %scatter_custom_fusion = f32[4096,128]{1,0:T(8,128)S(1)} fusion(s32[4096]{0:T(1024)S(1)} %bitcast.83, f32[4096,128]{1,0:T(8,128)} %bitcast_multiply_fusion.5, f32[]{:T(128)} %constant.42.clone.1), kind=kCustom, calls=%fused_computation.40 | custom fusion | flops 524288 | bytes 2097664 | tf_op jit(solution)/shard_map/scatter-add | solution.py:64
  96.1 5.6 %all-reduce.9.cloned.1.call-done = (f32[128,128]{1,0:T(8,128)}, f32[4096,128]{1,0:T(8,128)}) async-done(((f32[128,128]{1,0:T(8,128)}, f32[4096,128]{1,0:T(8,128)}), (f32[128,128]{1,0:T(8,128)}, f32[4096,128]{1,0:T(8,128)})) %all-reduce.9.cloned.1.call-update) | async-done | bytes 2162704 | tf_op jit(solution)/shard_map/psum | solution.py:45
  105.3 23.6 %scatter_fusion = f32[4096,128]{1,0:T(8,128)S(1)} fusion(f32[4096,128]{1,0:T(8,128)S(1)} %scatter_custom_fusion, s32[4096]{0:T(1024)S(1)} %bitcast.67, f32[4096,128]{1,0:T(8,128)} %bitcast_multiply_fusion.3), kind=kCustom, calls=%fused_computation.3 | custom fusion | flops 524288 | bytes 6307840 | tf_op jit(solution)/shard_map/scatter-add | solution.py:64
  130.3 4.7 %pad_maximum_fusion = f32[32,256,128]{2,1,0:T(8,128)} fusion(f32[32,128,128]{2,1,0:T(8,128)} %all-to-all-done.1, f32[32,128,128]{2,1,0:T(8,128)} %copy-done.3), kind=kLoop, calls=%fused_computation.12 | loop fusion | flops 1048576 | bytes 8388608 | tf_op jit(solution)/shard_map/concatenate | solution.py:52
  135.0 54.1 %all-reduce.5.cloned.1.call-done = f32[4096,128]{1,0:T(8,128)} async-done(((f32[4096,128]{1,0:T(8,128)}), f32[4096,128]{1,0:T(8,128)}) %all-reduce.5.cloned.1.call-update) | async-done | bytes 2097168 | tf_op jit(solution)/shard_map/psum | solution.py:67
  189.0 4.0 convolution_subtract_fusion.1
  193.0 27.7 %gather_fusion = f32[8192,128]{1,0:T(8,128)} fusion(f32[4096,128]{1,0:T(8,128)S(1)} %convolution_subtract_fusion.1, s32[8192]{0:T(1024)S(1)} %broadcast_clamp_fusion), kind=kCustom, calls=%fused_computation | custom fusion | bytes 8421376 | tf_op jit(solution)/shard_map/gather | solution.py:71
  220.7 5.2 %fusion.1 = f32[8192]{0:T(1024)} fusion(f32[8192,128]{1,0:T(8,128)} %gather_fusion, f32[32,256,128]{2,1,0:T(8,128)} %pad_maximum_fusion), kind=kLoop, calls=%fused_computation.15 | loop fusion | flops 2088960 | bytes 8421376 | tf_op jit(solution)/shard_map/reduce_sum | solution.py:71
  226.0 7.7 %all-to-all-start.3 = ((f32[32,1,256]{2,1,0:T(1,128)}), f32[32,1,256]{2,1,0:T(1,128)S(1)}, u32[]{:S(2)}, u32[]{:S(2)}) async-start(f32[32,1,256]{2,1,0:T(1,128)} %bitcast.14), calls=%async_computation.3 | async-start | bytes 65536 | tf_op jit(solution)/shard_map/all_to_all | solution.py:72
  235.1 5.8 %all-to-all-done.3 = f32[32,1,256]{2,1,0:T(1,128)S(1)} async-done(((f32[32,1,256]{2,1,0:T(1,128)}), f32[32,1,256]{2,1,0:T(1,128)S(1)}, u32[]{:S(2)}, u32[]{:S(2)}) %all-to-all-start.3) | async-done | bytes 32800 | tf_op jit(solution)/shard_map/all_to_all | solution.py:72
  243.7 10.7 %all_to_all.52 = f32[32,1,256]{2,1,0:T(1,128)S(1)} all-to-all(f32[32,1,256]{2,1,0:T(1,128)S(1)} %bitcast.82), channel_id=1, replica_groups=mesh['space'=32,'shell'=4] {'space'}, dimensions={0} | all-to-all | bytes 65536 | tf_op jit(solution)/shard_map/all_to_all | solution.py:60
  258.3 23.2 %scatter_custom_fusion.2 = f32[4096,128]{1,0:T(8,128)S(1)} fusion(s32[4096]{0:T(1024)S(1)} %bitcast.84, f32[4096,128]{1,0:T(8,128)} %get-tuple-element.23, f32[]{:T(128)} %constant.42.clone.1), kind=kCustom, calls=%fused_computation.38 | custom fusion | flops 524288 | bytes 2097664 | tf_op jit(solution)/shard_map/scatter-add | solution.py:64
  281.4 23.4 %scatter_fusion.1 = f32[4096,128]{1,0:T(8,128)S(1)} fusion(f32[4096,128]{1,0:T(8,128)S(1)} %scatter_custom_fusion.2, s32[4096]{0:T(1024)S(1)} %bitcast.68, f32[4096,128]{1,0:T(8,128)} %get-tuple-element.22), kind=kCustom, calls=%fused_computation.5 | custom fusion | flops 524288 | bytes 6307840 | tf_op jit(solution)/shard_map/scatter-add | solution.py:64
  306.2 54.9 %all-reduce.7.cloned.1.call-done = f32[4096,128]{1,0:T(8,128)} async-done(((f32[4096,128]{1,0:T(8,128)}), f32[4096,128]{1,0:T(8,128)}) %all-reduce.7.cloned.1.call-update) | async-done | bytes 2097168 | tf_op jit(solution)/shard_map/psum | solution.py:67
  361.2 4.0 convolution_subtract_fusion
  365.2 27.7 %gather_fusion.1 = f32[8192,128]{1,0:T(8,128)} fusion(f32[4096,128]{1,0:T(8,128)S(1)} %convolution_subtract_fusion, s32[8192]{0:T(1024)S(1)} %broadcast_clamp_fusion), kind=kCustom, calls=%fused_computation.1 | custom fusion | bytes 8421376 | tf_op jit(solution)/shard_map/gather | solution.py:71
  392.9 5.4 %fusion.2 = f32[8192]{0:T(1024)} fusion(f32[8192,128]{1,0:T(8,128)} %gather_fusion.1, f32[32,256,128]{2,1,0:T(8,128)} %pad_maximum_fusion), kind=kLoop, calls=%fused_computation.16 | loop fusion | flops 2088960 | bytes 8421376 | tf_op jit(solution)/shard_map/reduce_sum | solution.py:71
  398.2 7.5 %all-to-all-start.5 = ((f32[32,1,256]{2,1,0:T(1,128)}), f32[32,1,256]{2,1,0:T(1,128)S(1)}, u32[]{:S(2)}, u32[]{:S(2)}) async-start(f32[32,1,256]{2,1,0:T(1,128)} %bitcast.19), calls=%async_computation.5 | async-start | bytes 65536 | tf_op jit(solution)/shard_map/all_to_all | solution.py:72
  (62 shorter events, 35.7 us)
Async XLA Ops:
  7.2 26.4 %copy-start = (f32[128,64]{0,1:T(8,128)S(1)}, f32[128,64]{0,1:T(8,128)}, u32[]{:S(2)}) copy-start(f32[128,64]{0,1:T(8,128)} %param.12) | copy-start | bytes 98308
  7.2 12.0 %copy-start.10 = (s32[1,1,32]{2,1,0:T(1,128)S(1)}, s32[1,1,32]{2,1,0:T(1,128)}, u32[]{:S(2)}) copy-start(s32[1,1,32]{2,1,0:T(1,128)} %param.10) | copy-start | bytes 388
  10.6 15.8 %all-to-all-start.2 = ((f32[32,1,256]{2,1,0:T(1,128)}), f32[32,1,256]{2,1,0:T(1,128)S(1)}, u32[]{:S(2)}, u32[]{:S(2)}) async-start(f32[32,1,256]{2,1,0:T(1,128)} %bitcast.6), calls=%async_computation.2 | async-start | bytes 65536 | tf_op jit(solution)/shard_map/all_to_all | solution.py:60
  26.5 8.1 %copy-start.6 = (f32[64,4096]{1,0:T(8,128)S(1)}, f32[64,4096]{1,0:T(8,128)}, u32[]{:S(2)}) copy-start(f32[64,4096]{1,0:T(8,128)} %param.13) | copy-start | bytes 3145732
  26.5 34.9 %all-to-all-start = ((f32[32,128,128]{2,1,0:T(8,128)}), f32[32,128,128]{2,1,0:T(8,128)S(1)}, u32[]{:S(2)}, u32[]{:S(2)}) async-start(f32[32,128,128]{2,1,0:T(8,128)} %get-tuple-element.12), calls=%async_computation | async-start | bytes 4194304 | tf_op jit(solution)/shard_map/all_to_all | solution.py:42
  33.6 68.2 %all-reduce.9.cloned.1.call-start = ((), (), s32[]{:S(2)}) async-start(), calls=%async_computation.8 | async-start | bytes 4325376 | tf_op jit(solution)/shard_map/psum | solution.py:45
  34.5 4.8 %copy-start.8 = (s32[1,1,32,256]{3,2,1,0:T(8,128)S(1)}, s32[1,1,32,256]{3,2,1,0:T(8,128)}, u32[]{:S(2)}) copy-start(s32[1,1,32,256]{3,2,1,0:T(8,128)} %param.11) | copy-start | bytes 98308
  61.4 6.8 %copy-start.3 = (f32[32,128,128]{2,1,0:T(8,128)}, f32[32,128,128]{2,1,0:T(8,128)S(1)}, u32[]{:S(2)}) copy-start(f32[32,128,128]{2,1,0:T(8,128)S(1)} %all-to-all-done) | copy-start | bytes 6291460
  61.4 34.7 %all-to-all-start.1 = ((f32[32,128,128]{2,1,0:T(8,128)}), f32[32,128,128]{2,1,0:T(8,128)}, u32[]{:S(2)}, u32[]{:S(2)}) async-start(f32[32,128,128]{2,1,0:T(8,128)} %get-tuple-element.13), calls=%async_computation.1 | async-start | bytes 4194304 | tf_op jit(solution)/shard_map/all_to_all | solution.py:42
  68.1 120.9 %all-reduce.5.cloned.1.call-start = ((), (), s32[]{:S(2)}) async-start(), calls=%async_computation.6 | async-start | bytes 4194304 | tf_op jit(solution)/shard_map/psum | solution.py:67
  128.9 1.3 copy-start.1
  130.3 58.7 %copy-start.7 = (f32[128,128]{1,0:T(8,128)S(1)}, f32[128,128]{1,0:T(8,128)}, u32[]{:S(2)}) copy-start(f32[128,128]{1,0:T(8,128)} %get-tuple-element.6) | copy-start | bytes 196612
  226.0 16.4 %copy-start.9 = (f32[2048]{0:T(1024)S(1)}, f32[2048]{0:T(1024)}, u32[]{:S(2)}) copy-start(f32[2048]{0:T(1024)} %param.7) | copy-start | bytes 24580
  226.0 14.9 %all-to-all-start.3 = ((f32[32,1,256]{2,1,0:T(1,128)}), f32[32,1,256]{2,1,0:T(1,128)S(1)}, u32[]{:S(2)}, u32[]{:S(2)}) async-start(f32[32,1,256]{2,1,0:T(1,128)} %bitcast.14), calls=%async_computation.3 | async-start | bytes 65536 | tf_op jit(solution)/shard_map/all_to_all | solution.py:72
  233.6 127.5 %all-reduce.7.cloned.1.call-start = ((), (), s32[]{:S(2)}) async-start(), calls=%async_computation.7 | async-start | bytes 4194304 | tf_op jit(solution)/shard_map/psum | solution.py:67
  240.9 13.6 %copy-start.4 = (f32[32,128,128]{2,1,0:T(8,128)S(1)}, f32[32,128,128]{2,1,0:T(8,128)}, u32[]{:S(2)}) copy-start(f32[32,128,128]{2,1,0:T(8,128)} %copy-done.3) | copy-start | bytes 6291460
  304.9 1.3 copy-start.2
  392.9 12.9 %copy-start.5 = (f32[4096,128]{1,0:T(8,128)S(1)}, f32[4096,128]{1,0:T(8,128)}, u32[]{:S(2)}) copy-start(f32[4096,128]{1,0:T(8,128)} %all-reduce.7.cloned.1.call-done) | copy-start | bytes 6291460
  398.2 14.8 %all-to-all-start.5 = ((f32[32,1,256]{2,1,0:T(1,128)}), f32[32,1,256]{2,1,0:T(1,128)S(1)}, u32[]{:S(2)}, u32[]{:S(2)}) async-start(f32[32,1,256]{2,1,0:T(1,128)} %bitcast.19), calls=%async_computation.5 | async-start | bytes 65536 | tf_op jit(solution)/shard_map/all_to_all | solution.py:72
Sparse Core Ops, SparseCore 0:
  39.4 62.2 all-reduce.8
  130.4 58.6 all-reduce.4
  306.3 54.7 all-reduce.6
where the time goes:
time: 422 us
  waiting for transfers between devices  149 us (35%)
  other arithmetic  123 us (29%)
  local copies, waits for them, and re-layouts  62.1 us (15%)
  starting transfers between devices  37.7 us (9%)
  matrix products  24.4 us (6%)
  between operations  14 us (3%)
  blocking collectives  10.7 us (3%)
    psum x2, waiting for transfers between devices, on_device(): coeff_sum = lax.psum(partial_coeff, 'shell')  109 us
    scatter-add x4, other arithmetic, on_device(): partial_coeff.at[vox_parts[h]]  93.4 us
    gather x2, local copies, waits for them, and re-layouts, on_device(): adjoint[voxel_index]  55.4 us
    all_to_all x2, waiting for transfers between devices, on_device(): lax.all_to_all(masked[:, h * half:(h + 1) * half], 'space', 0, 0, tiled=T...  24.7 us
    all_to_all x2, starting transfers between devices, on_device(): lax.all_to_all(local_grad, 'space', split_axis=0, concat_axis=0, tiled=True)  15.2 us
    all_to_all x2, starting transfers between devices, on_device(): lax.all_to_all(masked[:, h * half:(h + 1) * half], 'space', 0, 0, tiled=T...  13.8 us
    all_to_all x1, blocking collectives, on_device(): lax.all_to_all(picked, 'space', split_axis=0, concat_axis=0, tiled=True)  10.7 us
    reduce_sum x2, other arithmetic, on_device(): jnp.sum(local_feat * adjoint[voxel_index], axis=1).reshape(blocks, slots)  10.6 us
  transfers between devices with their start and end apart: 8, of which 8 were waited for; matrix products, arithmetic and copies ran while one was open for 11% of the time, Pallas kernels for 0%

commit v1 on v0

--- a/solution.py
+++ b/solution.py
@@ -64,7 +64,7 @@
             partial_coeff = partial_coeff.at[vox_parts[h]].add(
                 part_x * feat_parts[h].reshape(-1, coeffs)
             )
-        coeff_sum = lax.psum(partial_coeff, "shell")
+        coeff_sum = jnp.sum(lax.all_gather(partial_coeff, "shell"), axis=0)
         if iteration == ITERS - 1:
             residual = jnp.einsum("jg,vj->gv", dictionary, coeff_sum, precision=HI) - measured
         adjoint = jnp.dot(coeff_sum, gram, precision=HI) - data_proj

time: 422 us -> 483 us (1.14)
  waiting for transfers between devices: 149 us -> 199 us
  other arithmetic: 123 us -> 134 us
    all_gather x0 -> x2, waiting for transfers between devices: none -> 159 us  [on_device(): coeff_sum = jnp.sum(lax.all_gather(partial_coeff, 'shell'), axis=0)]
    psum x2 -> x0, waiting for transfers between devices: 109 us -> none  [on_device(): coeff_sum = lax.psum(partial_coeff, 'shell')]
    reduce_sum x0 -> x2, other arithmetic: none -> 10.7 us  [on_device(): coeff_sum = jnp.sum(lax.all_gather(partial_coeff, 'shell'), axis=0)]
  transfers between devices with their start and end apart: 8 -> 8, of which waited for: 8 -> 8; matrix products, arithmetic and copies ran while one was open for 11% -> 10% of each run, Pallas kernels for 0% -> 0%
where the time goes in v1:
time: 483 us; the launch traced here: 482 us
  waiting for transfers between devices  199 us (41%)
  other arithmetic  134 us (28%)
  local copies, waits for them, and re-layouts  62.2 us (13%)
  starting transfers between devices  37.8 us (8%)
  matrix products  24.4 us (5%)
  between operations  14 us (3%)
  blocking collectives  10.7 us (2%)
    all_gather x2, waiting for transfers between devices, on_device(): coeff_sum = jnp.sum(lax.all_gather(partial_coeff, 'shell'), axis=0)  159 us
    scatter-add x4, other arithmetic, on_device(): partial_coeff.at[vox_parts[h]]  93.4 us
    gather x2, local copies, waits for them, and re-layouts, on_device(): adjoint[voxel_index]  55.5 us
    all_to_all x2, waiting for transfers between devices, on_device(): lax.all_to_all(masked[:, h * half:(h + 1) * half], 'space', 0, 0, tiled=T...  24.8 us
    all_to_all x2, starting transfers between devices, on_device(): lax.all_to_all(local_grad, 'space', split_axis=0, concat_axis=0, tiled=True)  15.3 us
    all_to_all x2, starting transfers between devices, on_device(): lax.all_to_all(masked[:, h * half:(h + 1) * half], 'space', 0, 0, tiled=T...  13.8 us
    all_to_all x1, blocking collectives, on_device(): lax.all_to_all(picked, 'space', split_axis=0, concat_axis=0, tiled=True)  10.7 us
    reduce_sum x2, other arithmetic, on_device(): coeff_sum = jnp.sum(lax.all_gather(partial_coeff, 'shell'), axis=0)  10.7 us
  transfers between devices with their start and end apart: 8, of which 8 were waited for; matrix products, arithmetic and copies ran while one was open for 10% of the time, Pallas kernels for 0%

profile of v1, /device:TPU:1, one launch (start us, length us, event | category | flops | bytes accessed | tf_op | source)
XLA Modules:
  0.0 482.3 jit_solution(16653392294861999275)
XLA Ops:
  10.6 8.6 %all-to-all-start.2 = ((f32[32,1,256]{2,1,0:T(1,128)}), f32[32,1,256]{2,1,0:T(1,128)S(1)}, u32[]{:S(2)}, u32[]{:S(2)}) async-start(f32[32,1,256]{2,1,0:T(1,128)} %bitcast.6), calls=%async_computation.2 | async-start | bytes 65536 | tf_op jit(solution)/shard_map/all_to_all | solution.py:60
  19.3 4.5 multiply_reduce_fusion
  26.5 7.1 %all-to-all-start = ((f32[32,128,128]{2,1,0:T(8,128)}), f32[32,128,128]{2,1,0:T(8,128)S(1)}, u32[]{:S(2)}, u32[]{:S(2)}) async-start(f32[32,128,128]{2,1,0:T(8,128)} %get-tuple-element.12), calls=%async_computation | async-start | bytes 4194304 | tf_op jit(solution)/shard_map/all_to_all | solution.py:42
  34.5 4.8 fusion.49
  39.4 22.0 %all-to-all-done = f32[32,128,128]{2,1,0:T(8,128)S(1)} async-done(((f32[32,128,128]{2,1,0:T(8,128)}), f32[32,128,128]{2,1,0:T(8,128)S(1)}, u32[]{:S(2)}, u32[]{:S(2)}) %all-to-all-start) | async-done | bytes 2097184 | tf_op jit(solution)/shard_map/all_to_all | solution.py:42
  61.4 6.7 %all-to-all-start.1 = ((f32[32,128,128]{2,1,0:T(8,128)}), f32[32,128,128]{2,1,0:T(8,128)}, u32[]{:S(2)}, u32[]{:S(2)}) async-start(f32[32,128,128]{2,1,0:T(8,128)} %get-tuple-element.13), calls=%async_computation.1 | async-start | bytes 4194304 | tf_op jit(solution)/shard_map/all_to_all | solution.py:42
  70.2 23.2 %scatter_custom_fusion = f32[4096,128]{1,0:T(8,128)S(1)} fusion(s32[4096]{0:T(1024)S(1)} %bitcast.87, f32[4096,128]{1,0:T(8,128)} %bitcast_multiply_fusion.5, f32[]{:T(128)} %constant.42.clone.1), kind=kCustom, calls=%fused_computation.40 | custom fusion | flops 524288 | bytes 2097664 | tf_op jit(solution)/shard_map/scatter-add | solution.py:64
  96.1 5.6 %all-reduce.3.cloned.1.call-done = (f32[128,128]{1,0:T(8,128)}, f32[4096,128]{1,0:T(8,128)}) async-done(((f32[128,128]{1,0:T(8,128)}, f32[4096,128]{1,0:T(8,128)}), (f32[128,128]{1,0:T(8,128)}, f32[4096,128]{1,0:T(8,128)})) %all-reduce.3.cloned.1.call-update) | async-done | bytes 2162704 | tf_op jit(solution)/shard_map/psum | solution.py:45
  105.3 23.6 %scatter_fusion = f32[4096,128]{1,0:T(8,128)S(1)} fusion(f32[4096,128]{1,0:T(8,128)S(1)} %scatter_custom_fusion, s32[4096]{0:T(1024)S(1)} %bitcast.71, f32[4096,128]{1,0:T(8,128)} %bitcast_multiply_fusion.3), kind=kCustom, calls=%fused_computation.3 | custom fusion | flops 524288 | bytes 6307840 | tf_op jit(solution)/shard_map/scatter-add | solution.py:64
  130.3 4.6 pad_maximum_fusion
  135.0 78.3 %all-gather.5.cloned.1.call-done = f32[16384,128]{1,0:T(8,128)} async-done(((f32[4096,128]{1,0:T(8,128)}), f32[16384,128]{1,0:T(8,128)}) %all-gather.5.cloned.1.call-update) | async-done | bytes 8388624 | tf_op jit(solution)/shard_map/all_gather | solution.py:67
  213.3 5.4 %reduce_sum.65 = f32[4096,128]{1,0:T(8,128)} reduce(f32[4,4096,128]{2,1,0:T(8,128)} %bitcast.69, f32[]{:T(128)} %constant.42.clone.1), dimensions={0}, to_apply=%region_6.7 | reduce | flops 1572864 | bytes 10485764 | tf_op jit(solution)/shard_map/reduce_sum | solution.py:67
  222.7 27.8 %gather_fusion = f32[8192,128]{1,0:T(8,128)} fusion(f32[4096,128]{1,0:T(8,128)S(1)} %convolution_subtract_fusion.1, s32[8192]{0:T(1024)S(1)} %broadcast_clamp_fusion), kind=kCustom, calls=%fused_computation | custom fusion | bytes 8421376 | tf_op jit(solution)/shard_map/gather | solution.py:71
  250.5 5.2 %fusion.1 = f32[8192]{0:T(1024)} fusion(f32[8192,128]{1,0:T(8,128)} %gather_fusion, f32[32,256,128]{2,1,0:T(8,128)} %pad_maximum_fusion), kind=kLoop, calls=%fused_computation.15 | loop fusion | flops 2088960 | bytes 8421376 | tf_op jit(solution)/shard_map/reduce_sum | solution.py:71
  255.7 7.7 %all-to-all-start.3 = ((f32[32,1,256]{2,1,0:T(1,128)}), f32[32,1,256]{2,1,0:T(1,128)S(1)}, u32[]{:S(2)}, u32[]{:S(2)}) async-start(f32[32,1,256]{2,1,0:T(1,128)} %bitcast.15), calls=%async_computation.3 | async-start | bytes 65536 | tf_op jit(solution)/shard_map/all_to_all | solution.py:72
  264.9 5.8 %all-to-all-done.3 = f32[32,1,256]{2,1,0:T(1,128)S(1)} async-done(((f32[32,1,256]{2,1,0:T(1,128)}), f32[32,1,256]{2,1,0:T(1,128)S(1)}, u32[]{:S(2)}, u32[]{:S(2)}) %all-to-all-start.3) | async-done | bytes 32800 | tf_op jit(solution)/shard_map/all_to_all | solution.py:72
  273.5 10.7 %all_to_all.52 = f32[32,1,256]{2,1,0:T(1,128)S(1)} all-to-all(f32[32,1,256]{2,1,0:T(1,128)S(1)} %bitcast.86), channel_id=1, replica_groups=mesh['space'=32,'shell'=4] {'space'}, dimensions={0} | all-to-all | bytes 65536 | tf_op jit(solution)/shard_map/all_to_all | solution.py:60
  288.0 23.2 %scatter_custom_fusion.2 = f32[4096,128]{1,0:T(8,128)S(1)} fusion(s32[4096]{0:T(1024)S(1)} %bitcast.88, f32[4096,128]{1,0:T(8,128)} %get-tuple-element.23, f32[]{:T(128)} %constant.42.clone.1), kind=kCustom, calls=%fused_computation.38 | custom fusion | flops 524288 | bytes 2097664 | tf_op jit(solution)/shard_map/scatter-add | solution.py:64
  311.2 23.4 %scatter_fusion.1 = f32[4096,128]{1,0:T(8,128)S(1)} fusion(f32[4096,128]{1,0:T(8,128)S(1)} %scatter_custom_fusion.2, s32[4096]{0:T(1024)S(1)} %bitcast.72, f32[4096,128]{1,0:T(8,128)} %get-tuple-element.22), kind=kCustom, calls=%fused_computation.5 | custom fusion | flops 524288 | bytes 6307840 | tf_op jit(solution)/shard_map/scatter-add | solution.py:64
  335.9 80.4 %all-gather.7.cloned.1.call-done = f32[16384,128]{1,0:T(8,128)} async-done(((f32[4096,128]{1,0:T(8,128)}), f32[16384,128]{1,0:T(8,128)}) %all-gather.7.cloned.1.call-update) | async-done | bytes 8388624 | tf_op jit(solution)/shard_map/all_gather | solution.py:67
  416.4 5.4 %reduce_sum.68 = f32[4096,128]{1,0:T(8,128)} reduce(f32[4,4096,128]{2,1,0:T(8,128)} %bitcast.70, f32[]{:T(128)} %constant.42.clone.1), dimensions={0}, to_apply=%region_11.12 | reduce | flops 1572864 | bytes 10485764 | tf_op jit(solution)/shard_map/reduce_sum | solution.py:67
  425.8 27.8 %gather_fusion.1 = f32[8192,128]{1,0:T(8,128)} fusion(f32[4096,128]{1,0:T(8,128)S(1)} %convolution_subtract_fusion, s32[8192]{0:T(1024)S(1)} %broadcast_clamp_fusion), kind=kCustom, calls=%fused_computation.1 | custom fusion | bytes 8421376 | tf_op jit(solution)/shard_map/gather | solution.py:71
  453.5 5.4 %fusion.2 = f32[8192]{0:T(1024)} fusion(f32[8192,128]{1,0:T(8,128)} %gather_fusion.1, f32[32,256,128]{2,1,0:T(8,128)} %pad_maximum_fusion), kind=kLoop, calls=%fused_computation.16 | loop fusion | flops 2088960 | bytes 8421376 | tf_op jit(solution)/shard_map/reduce_sum | solution.py:71
  458.9 7.6 %all-to-all-start.5 = ((f32[32,1,256]{2,1,0:T(1,128)}), f32[32,1,256]{2,1,0:T(1,128)S(1)}, u32[]{:S(2)}, u32[]{:S(2)}) async-start(f32[32,1,256]{2,1,0:T(1,128)} %bitcast.21), calls=%async_computation.5 | async-start | bytes 65536 | tf_op jit(solution)/shard_map/all_to_all | solution.py:72
  (64 shorter events, 43.6 us)
Async XLA Ops:
  7.2 26.4 %copy-start = (f32[128,64]{0,1:T(8,128)S(1)}, f32[128,64]{0,1:T(8,128)}, u32[]{:S(2)}) copy-start(f32[128,64]{0,1:T(8,128)} %param.12) | copy-start | bytes 98308
  7.2 12.0 %copy-start.10 = (s32[1,1,32]{2,1,0:T(1,128)S(1)}, s32[1,1,32]{2,1,0:T(1,128)}, u32[]{:S(2)}) copy-start(s32[1,1,32]{2,1,0:T(1,128)} %param.10) | copy-start | bytes 388
  10.6 15.8 %all-to-all-start.2 = ((f32[32,1,256]{2,1,0:T(1,128)}), f32[32,1,256]{2,1,0:T(1,128)S(1)}, u32[]{:S(2)}, u32[]{:S(2)}) async-start(f32[32,1,256]{2,1,0:T(1,128)} %bitcast.6), calls=%async_computation.2 | async-start | bytes 65536 | tf_op jit(solution)/shard_map/all_to_all | solution.py:60
  26.5 8.1 %copy-start.6 = (f32[64,4096]{1,0:T(8,128)S(1)}, f32[64,4096]{1,0:T(8,128)}, u32[]{:S(2)}) copy-start(f32[64,4096]{1,0:T(8,128)} %param.13) | copy-start | bytes 3145732
  26.5 34.9 %all-to-all-start = ((f32[32,128,128]{2,1,0:T(8,128)}), f32[32,128,128]{2,1,0:T(8,128)S(1)}, u32[]{:S(2)}, u32[]{:S(2)}) async-start(f32[32,128,128]{2,1,0:T(8,128)} %get-tuple-element.12), calls=%async_computation | async-start | bytes 4194304 | tf_op jit(solution)/shard_map/all_to_all | solution.py:42
  33.6 68.2 %all-reduce.3.cloned.1.call-start = ((), (), s32[]{:S(2)}) async-start(), calls=%async_computation.8 | async-start | bytes 4325376 | tf_op jit(solution)/shard_map/psum | solution.py:45
  34.5 4.8 copy-start.8
  61.4 6.8 %copy-start.3 = (f32[32,128,128]{2,1,0:T(8,128)}, f32[32,128,128]{2,1,0:T(8,128)S(1)}, u32[]{:S(2)}) copy-start(f32[32,128,128]{2,1,0:T(8,128)S(1)} %all-to-all-done) | copy-start | bytes 6291460
  61.4 34.7 %all-to-all-start.1 = ((f32[32,128,128]{2,1,0:T(8,128)}), f32[32,128,128]{2,1,0:T(8,128)}, u32[]{:S(2)}, u32[]{:S(2)}) async-start(f32[32,128,128]{2,1,0:T(8,128)} %get-tuple-element.13), calls=%async_computation.1 | async-start | bytes 4194304 | tf_op jit(solution)/shard_map/all_to_all | solution.py:42
  68.1 145.2 %all-gather.5.cloned.1.call-start = ((), (), s32[]{:S(2)}) async-start(), calls=%async_computation.6 | async-start | bytes 10485760 | tf_op jit(solution)/shard_map/all_gather | solution.py:67
  128.9 1.3 copy-start.1
  213.3 5.4 %copy-start.7 = (f32[128,128]{1,0:T(8,128)S(1)}, f32[128,128]{1,0:T(8,128)}, u32[]{:S(2)}) copy-start(f32[128,128]{1,0:T(8,128)} %get-tuple-element.6) | copy-start | bytes 196612
  255.7 16.4 %copy-start.9 = (f32[2048]{0:T(1024)S(1)}, f32[2048]{0:T(1024)}, u32[]{:S(2)}) copy-start(f32[2048]{0:T(1024)} %param.7) | copy-start | bytes 24580
  255.7 15.0 %all-to-all-start.3 = ((f32[32,1,256]{2,1,0:T(1,128)}), f32[32,1,256]{2,1,0:T(1,128)S(1)}, u32[]{:S(2)}, u32[]{:S(2)}) async-start(f32[32,1,256]{2,1,0:T(1,128)} %bitcast.15), calls=%async_computation.3 | async-start | bytes 65536 | tf_op jit(solution)/shard_map/all_to_all | solution.py:72
  263.4 153.0 %all-gather.7.cloned.1.call-start = ((), (), s32[]{:S(2)}) async-start(), calls=%async_computation.7 | async-start | bytes 10485760 | tf_op jit(solution)/shard_map/all_gather | solution.py:67
  270.7 13.6 %copy-start.4 = (f32[32,128,128]{2,1,0:T(8,128)S(1)}, f32[32,128,128]{2,1,0:T(8,128)}, u32[]{:S(2)}) copy-start(f32[32,128,128]{2,1,0:T(8,128)} %copy-done.3) | copy-start | bytes 6291460
  334.6 1.3 copy-start.2
  453.5 12.9 %copy-start.5 = (f32[4096,128]{1,0:T(8,128)S(1)}, f32[4096,128]{1,0:T(8,128)}, u32[]{:S(2)}) copy-start(f32[4096,128]{1,0:T(8,128)} %reduce_sum.68) | copy-start | bytes 6291460
  458.9 14.8 %all-to-all-start.5 = ((f32[32,1,256]{2,1,0:T(1,128)}), f32[32,1,256]{2,1,0:T(1,128)S(1)}, u32[]{:S(2)}, u32[]{:S(2)}) async-start(f32[32,1,256]{2,1,0:T(1,128)} %bitcast.21), calls=%async_computation.5 | async-start | bytes 65536 | tf_op jit(solution)/shard_map/all_to_all | solution.py:72
Sparse Core Ops, SparseCore 0:
  39.5 62.2 all-reduce.2
  130.3 82.9 all-gather.4
  336.1 80.2 all-gather.6
